TPU v7x, 32 devices: a whole 2x2x4 slice. The times are simulated.
32 devices in a mesh: dp: 8 (over z, y), feat: 4 (over x, core).
Axes of the slice: x: 2, y: 2, z: 4, core: 2. Of those that a mesh axis runs over, the one named last changes fastest.
Arguments:
- activations: bfloat16 [16384, 2048], P('feat', 'dp'), may hold values from -6 to 6
- cotangent: bfloat16 [16384, 2048], P('feat', 'dp'), may hold values from -6 to 6
- r_mix: bfloat16 [64, 256, 256], P('feat', 'dp'), may hold values from -0.375 to 0.375
- l_mix: bfloat16 [256, 4096], P('feat', 'dp'), may hold values from -0.75 to 0.75
Outputs:
- grad_x: bfloat16 [16384, 2048], P('feat', 'dp')
- grad_r: float32 [64, 256, 256], P('feat', 'dp')
- grad_l: float32 [256, 4096], P('feat', 'dp')
All inputs are finite; a program needn't handle non-finite values.
Results may differ from a plain program's by a relative error of at most 0.0055.
Values may be sent and summed in bfloat16 or wider, within the bound.
No kernel may reach another device: no remote copies, remote signals or barrier semaphores. Data moves between devices by JAX's collectives and lax.ppermute only.
A program may use at most 64 MiB of HBM per device.

v0:
```python
import math
import jax
import jax.numpy as jnp
from jax import lax
from jax.sharding import PartitionSpec as P

BLOCKS = 64
WIDTH = 256


def gelu_tanh(values):
    return jax.nn.gelu(values, approximate=True)


def slope_of(pre_act, upstream):
    _, pullback = jax.vjp(gelu_tanh, pre_act)
    return pullback(upstream.astype(jnp.float32))[0].astype(jnp.bfloat16)


def body(activations, cotangent, r_mix, l_mix):
    tok_count = activations.shape[1]
    local_blocks = activations.shape[0] // WIDTH
    grad_scale = 1.0 / math.sqrt(tok_count * lax.axis_size("dp"))
    r_whole, l_whole = (
        lax.all_gather(r_mix, "dp", axis=1, tiled=True),
        lax.all_gather(l_mix, "dp", axis=1, tiled=True),
    )
    local_cols = l_whole.shape[0]
    l_blocks = l_whole.reshape(local_cols, BLOCKS, BLOCKS)
    x_blocks = activations.reshape(local_blocks, WIDTH, tok_count)
    g_blocks = cotangent.reshape(local_blocks, WIDTH, tok_count)
    mixed_rows = jnp.einsum(
        "bit,bio->bot", x_blocks, r_whole, preferred_element_type=jnp.float32
    ).astype(jnp.bfloat16)
    outgoing = (mixed_rows,)
    parts = (lax.all_to_all(outgoing[0], "feat", split_axis=1, concat_axis=0, tiled=True),)
    columns = parts[0]
    pre_act = jnp.einsum("bst,sbc->cst", columns, l_blocks, preferred_element_type=jnp.float32)
    arrived = (columns, pre_act) + tuple(parts[1:])
    columns = arrived[0]
    pre_act = arrived[1]
    pre_rows = lax.all_to_all(pre_act, "feat", split_axis=0, concat_axis=1, tiled=True)
    slope_rows = slope_of(pre_rows, g_blocks)
    slope_cols = lax.all_to_all(slope_rows, "feat", split_axis=1, concat_axis=0, tiled=True)
    back_cols = jnp.einsum(
        "cst,sbc->bst", slope_cols, l_blocks, preferred_element_type=jnp.float32
    ).astype(jnp.bfloat16)
    l_term = jnp.einsum("bst,cst->sbc", columns, slope_cols, preferred_element_type=jnp.float32)
    l_term = l_term.reshape(local_cols, BLOCKS * BLOCKS) * grad_scale
    back_rows = lax.all_to_all(back_cols, "feat", split_axis=0, concat_axis=1, tiled=True)
    back_rows, through_r = (
        back_rows,
        jnp.einsum("bot,bio->bit", back_rows, r_whole, preferred_element_type=jnp.float32),
    )
    grad_x = (
        (g_blocks.astype(jnp.float32) + through_r)
        .astype(jnp.bfloat16)
        .reshape(local_blocks * WIDTH, tok_count)
    )
    r_term = (
        jnp.einsum("bit,bot->bio", x_blocks, back_rows, preferred_element_type=jnp.float32)
        * grad_scale
    )
    grad_l, grad_r = (
        lax.psum_scatter(l_term, "dp", scatter_dimension=1, tiled=True),
        lax.psum_scatter(r_term, "dp", scatter_dimension=1, tiled=True),
    )
    return (grad_x, grad_r, grad_l)


def solution(mesh):
    placed = (P("feat", "dp"), P("feat", "dp"), P("feat", "dp", None), P("feat", "dp"))
    return jax.shard_map(
        body,
        mesh=mesh,
        in_specs=placed,
        out_specs=(P("feat", "dp"), P("feat", "dp", None), P("feat", "dp")),
        check_vma=False,
    )
```

profile of v0, /device:TPU:0, one launch (start us, length us, event | category | flops | bytes accessed | tf_op | source)
XLA Modules:
  0.0 399.9 jit_solution(9625601833998472881)
XLA Ops:
  7.2 0.7 all-gather.2.cloned.1.call-update
  7.9 54.3 %all-gather.2.cloned.1.call-done = bf16[16,256,256]{2,1,0:T(8,128)(2,1)} async-done(((bf16[16,32,256]{2,1,0:T(8,128)(2,1)}), bf16[16,256,256]{2,1,0:T(8,128)(2,1)}) %all-gather.2.cloned.1.call-update) | async-done | bytes 2097168 | tf_op jit(solution)/shard_map/all_gather | solution.py:25
  62.2 2.4 convolution_convert_fusion
  64.6 2.5 copy.19
  67.1 4.6 %all-to-all-start = ((bf16[16,256,256]{2,0,1:T(8,128)(2,1)}), bf16[16,256,256]{2,0,1:T(8,128)(2,1)}, u32[]{:S(2)}, u32[]{:S(2)}) async-start(bf16[16,256,256]{2,0,1:T(8,128)(2,1)} %copy.19), calls=%async_computation | async-start | bytes 4194304 | tf_op jit(solution)/shard_map/all_to_all | solution.py:36
  71.7 33.3 %all_gather.7 = bf16[64,4096]{1,0:T(8,128)(2,1)} all-gather(bf16[64,512]{1,0:T(8,128)(2,1)S(1)} %copy-done.5), channel_id=1, replica_groups=mesh['dp'=8,'feat'=4] {'dp'}, dimensions={1}, use_global_device_ids=true | all-gather | bytes 589824 | tf_op jit(solution)/shard_map/all_gather | solution.py:26
  105.0 2.1 reshape.22
  107.1 1.8 copy.20
  109.0 1.3 copy-done.1
  110.3 0.8 convolution_bitcast_fusion
  111.0 2.4 copy.22
  113.5 51.1 %all_to_all.72 = f32[64,64,256]{2,1,0:T(8,128)S(1)} all-to-all(f32[64,64,256]{2,1,0:T(8,128)S(1)} %copy.22), channel_id=1, replica_groups=mesh['dp'=8,'feat'=4] {'feat'}, dimensions={0} | all-to-all | bytes 8388608 | tf_op jit(solution)/shard_map/all_to_all | solution.py:42
  164.6 0.5 copy.23
  165.0 1.1 copy-done.4
  166.1 3.3 fusion.6
  169.5 1.2 copy.24
  170.6 28.2 %all_to_all.73 = bf16[16,256,256]{2,0,1:T(8,128)(2,1)S(1)} all-to-all(bf16[16,256,256]{2,0,1:T(8,128)(2,1)S(1)} %copy.24), channel_id=1, replica_groups=mesh['dp'=8,'feat'=4] {'feat'}, dimensions={1} | all-to-all | bytes 4194304 | tf_op jit(solution)/shard_map/all_to_all | solution.py:44
  198.8 0.3 copy.25
  199.1 0.7 convert_bitcast_fusion
  199.8 0.6 copy-done.2
  200.4 1.2 copy.26
  201.6 28.2 %all_to_all.74 = bf16[64,64,256]{2,1,0:T(8,128)(2,1)S(1)} all-to-all(bf16[64,64,256]{2,1,0:T(8,128)(2,1)S(1)} %copy.26), channel_id=1, replica_groups=mesh['dp'=8,'feat'=4] {'feat'}, dimensions={0} | all-to-all | bytes 4194304 | tf_op jit(solution)/shard_map/all_to_all | solution.py:50
  229.8 0.2 copy.27
  230.0 1.3 copy-done.3
  231.4 2.7 multiply_bitcast_fusion
  234.1 5.5 %copy.28 = f32[16,256,256]{2,0,1:T(8,128)} copy(f32[16,256,256]{1,2,0:T(8,128)} %multiply_bitcast_fusion) | data formatting | bytes 8388608 | tf_op jit(solution)/shard_map/mul | solution.py:61
  239.6 4.2 %convolution_multiply_fusion = f32[64,64,64]{2,1,0:T(8,128)} fusion(bf16[64,64,256]{2,0,1:T(8,128)(2,1)} %bitcast.50, bf16[64,64,256]{2,0,1:T(8,128)(2,1)} %bitcast.52), kind=kOutput, calls=%fused_computation.20 | convolution fusion | flops 134479872 | bytes 5242880 | tf_op jit(solution)/shard_map/bst,cst->sbc/dot_general | solution.py:48
  243.9 3.1 mul.78
  247.0 4.9 %fusion.10 = bf16[16,256,256]{2,1,0:T(8,128)(2,1)} fusion(bf16[16,256,256]{2,1,0:T(8,128)(2,1)} %bitcast.58, bf16[16,256,256]{2,1,0:T(8,128)(2,1)} %all-gather.2.cloned.1.call-done, bf16[16,256,256]{2,1,0:T(8,128)(2,1)} %bitcast.54), kind=kOutput, calls=%fused_computation.15 | convolution fusion | flops 540016640 | bytes 8388608 | tf_op jit(solution)/shard_map/bot,bio->bit/dot_general | solution.py:53
  251.9 73.5 %reduce-scatter.3.cloned.1.call-done = f32[16,32,256]{2,0,1:T(8,128)} async-done(((f32[16,256,256]{2,0,1:T(8,128)}), f32[16,32,256]{2,0,1:T(8,128)}) %reduce-scatter.3.cloned.1.call-update) | async-done | bytes 524304 | tf_op jit(solution)/shard_map/reduce_scatter | solution.py:66
  325.4 2.1 copy.29
  327.6 65.8 %reduce-scatter.5.cloned.1.call-done = f32[64,512]{1,0:T(8,128)} async-done(((f32[64,4096]{1,0:T(8,128)}), f32[64,512]{1,0:T(8,128)}) %reduce-scatter.5.cloned.1.call-update) | async-done | bytes 131088 | tf_op jit(solution)/shard_map/reduce_scatter | solution.py:65
  (14 shorter events, 0.2 us)
Async XLA Ops:
  7.2 55.0 %copy-start = (bf16[4096,256]{1,0:T(8,128)(2,1)S(1)}, bf16[4096,256]{1,0:T(8,128)(2,1)}, u32[]{:S(2)}) copy-start(bf16[4096,256]{1,0:T(8,128)(2,1)} %param.4) | copy-start | bytes 6291460
  7.2 55.0 %all-gather.2.cloned.1.call-start = ((), (), s32[]{:S(2)}) async-start(), calls=%async_computation.6 | async-start | bytes 2359296 | tf_op jit(solution)/shard_map/all_gather | solution.py:25
  67.1 4.6 %copy-start.5 = (bf16[64,512]{1,0:T(8,128)(2,1)S(1)}, bf16[64,512]{1,0:T(8,128)(2,1)}, u32[]{:S(2)}) copy-start(bf16[64,512]{1,0:T(8,128)(2,1)} %param.7) | copy-start | bytes 196612
  67.1 40.0 %all-to-all-start = ((bf16[16,256,256]{2,0,1:T(8,128)(2,1)}), bf16[16,256,256]{2,0,1:T(8,128)(2,1)}, u32[]{:S(2)}, u32[]{:S(2)}) async-start(bf16[16,256,256]{2,0,1:T(8,128)(2,1)} %copy.19), calls=%async_computation | async-start | bytes 4194304 | tf_op jit(solution)/shard_map/all_to_all | solution.py:36
  71.6 253.8 %reduce-scatter.3.cloned.1.call-start = ((), (), s32[]{:S(2)}) async-start(), calls=%async_computation.7 | async-start | bytes 4718592 | tf_op jit(solution)/shard_map/reduce_scatter | solution.py:66
  109.0 1.3 copy-start.1
  164.6 1.6 copy-start.4
  199.1 1.3 copy-start.2
  230.0 1.3 copy-start.3
  239.6 153.8 %reduce-scatter.5.cloned.1.call-start = ((), (), s32[]{:S(2)}) async-start(), calls=%async_computation.8 | async-start | bytes 1179648 | tf_op jit(solution)/shard_map/reduce_scatter | solution.py:65
Sparse Core Ops, SparseCore 0:
  10.2 51.9 all-gather.1
  239.7 85.6 reduce-scatter.2
  329.8 63.5 reduce-scatter.4
where the time goes:
time: 401 us; the launch traced here: 400 us
  waiting for transfers between devices  194 us (48%)
  blocking collectives  141 us (35%)
  local copies, waits for them, and re-layouts  27.3 us (7%)
  matrix products  15.7 us (4%)
  between operations  13.9 us (3%)
  starting transfers between devices  4.69 us (1%)
    reduce_scatter x1, waiting for transfers between devices, body(): lax.psum_scatter(r_term, 'dp', scatter_dimension=1, tiled=True)  73.5 us
    reduce_scatter x1, waiting for transfers between devices, body(): lax.psum_scatter(l_term, 'dp', scatter_dimension=1, tiled=True)  65.8 us
    all_gather x1, waiting for transfers between devices, body(): lax.all_gather(r_mix, 'dp', axis=1, tiled=True)  54.3 us
    all_to_all x1, blocking collectives, body(): lax.all_to_all(pre_act, 'feat', split_axis=0, concat_axis=1, tiled=True)  51.1 us
    all_gather x1, blocking collectives, body(): lax.all_gather(l_mix, 'dp', axis=1, tiled=True)  33.3 us
    all_to_all x1, blocking collectives, body(): lax.all_to_all(slope_rows, 'feat', split_axis=1, concat_axis=0, tiled=True)  28.2 us
    all_to_all x1, blocking collectives, body(): lax.all_to_all(back_cols, 'feat', split_axis=0, concat_axis=1, tiled=True)  28.2 us
  transfers between devices with their start and end apart: 4, of which 3 were waited for; matrix products, arithmetic and copies ran while one was open for 4% of the time, Pallas kernels for 0%

commit v1 on v0

--- a/solution.py
+++ b/solution.py
@@ -6,6 +6,32 @@
 
 BLOCKS = 64
 WIDTH = 256
+
+
+def _shape_slots(z, axis_k):
+    z = jnp.moveaxis(z, 0, axis_k)
+    spare = z.shape
+    return z.reshape(*spare[:axis_k], spare[axis_k] * spare[axis_k + 1], *spare[axis_k + 2 :])
+
+
+def proceed_levels_all(local_x, axis_name, out_dim):
+    n_slots = lax.psum(1, axis_name)
+    windows = list(map(lambda dev: (dev, (dev + 1) % n_slots), range(n_slots)))
+    store = [(kk, nth) for nth, kk in windows]
+    block_next, p_next = ([], [])
+    to_i = 0
+    while to_i < n_slots - 1:
+        if to_i % 2 == 0:
+            block_next.append(
+                lax.ppermute(block_next[-1] if block_next else local_x, axis_name, windows)
+            )
+        else:
+            p_next.append(lax.ppermute(p_next[-1] if p_next else local_x, axis_name, store))
+        to_i += 1
+    finding = jnp.stack([*block_next[::-1], local_x, *p_next], axis=0)
+    f_next = lax.axis_index(axis_name) - len(block_next)
+    finding = finding[(jnp.arange(n_slots) - f_next) % n_slots]
+    return _shape_slots(finding, out_dim)
 
 
 def gelu_tanh(values):
@@ -23,7 +49,7 @@
     grad_scale = 1.0 / math.sqrt(tok_count * lax.axis_size("dp"))
     r_whole, l_whole = (
         lax.all_gather(r_mix, "dp", axis=1, tiled=True),
-        lax.all_gather(l_mix, "dp", axis=1, tiled=True),
+        proceed_levels_all(l_mix, "dp", 1),
     )
     local_cols = l_whole.shape[0]
     l_blocks = l_whole.reshape(local_cols, BLOCKS, BLOCKS)

time: 401 us -> 392 us (0.978)
  blocking collectives: 141 us -> 107 us
  starting transfers between devices: 4.69 us -> 22.7 us
  waiting for transfers between devices: 194 us -> 200 us
    all_gather x1 -> x0, blocking collectives: 33.3 us -> none  [body(): lax.all_gather(l_mix, 'dp', axis=1, tiled=True)]
    all_gather x1, waiting for transfers between devices: 54.3 us -> 25.5 us  [body(): lax.all_gather(r_mix, 'dp', axis=1, tiled=True)]
    all_to_all x1, waiting for transfers between devices: 0.01 us -> 22.3 us  [body(): lax.all_to_all(outgoing[0], 'feat', split_axis=1, concat_axis=0, tiled=True)]
    ppermute x0 -> x7, starting transfers between devices: none -> 18 us  [the longest x3 15 us: proceed_levels_all(): lax.ppermute(p_next[-1] if p_next else local_x, axis_name, store)]
    ppermute x0 -> x7, waiting for transfers between devices: none -> 12.7 us  [the longest x4 11.8 us: proceed_levels_all(): lax.ppermute(block_next[-1] if block_next else local_x, axis_name, windows)]
  transfers between devices with their start and end apart: 4 -> 11, of which waited for: 3 -> 9; matrix products, arithmetic and copies ran while one was open for 4% -> 6% of each run, Pallas kernels for 0% -> 0%
where the time goes in v1:
time: 392 us
  waiting for transfers between devices  200 us (51%)
  blocking collectives  107 us (27%)
  local copies, waits for them, and re-layouts  28.6 us (7%)
  starting transfers between devices  22.7 us (6%)
  matrix products  15.8 us (4%)
  between operations  14 us (4%)
    reduce_scatter x1, waiting for transfers between devices, body(): lax.psum_scatter(r_term, 'dp', scatter_dimension=1, tiled=True)  73.3 us
    reduce_scatter x1, waiting for transfers between devices, body(): lax.psum_scatter(l_term, 'dp', scatter_dimension=1, tiled=True)  65.8 us
    all_to_all x1, blocking collectives, body(): lax.all_to_all(pre_act, 'feat', split_axis=0, concat_axis=1, tiled=True)  50.7 us
    all_to_all x1, blocking collectives, body(): lax.all_to_all(slope_rows, 'feat', split_axis=1, concat_axis=0, tiled=True)  28.2 us
    all_to_all x1, blocking collectives, body(): lax.all_to_all(back_cols, 'feat', split_axis=0, concat_axis=1, tiled=True)  28.2 us
    all_gather x1, waiting for transfers between devices, body(): lax.all_gather(r_mix, 'dp', axis=1, tiled=True)  25.5 us
    all_to_all x1, waiting for transfers between devices, body(): lax.all_to_all(outgoing[0], 'feat', split_axis=1, concat_axis=0, tiled=True)  22.3 us
    ppermute x3, starting transfers between devices, proceed_levels_all(): lax.ppermute(p_next[-1] if p_next else local_x, axis_name, store)  15 us
  transfers between devices with their start and end apart: 11, of which 9 were waited for; matrix products, arithmetic and copies ran while one was open for 6% of the time, Pallas kernels for 0%

profile of v1, /device:TPU:0, one launch (start us, length us, event | category | flops | bytes accessed | tf_op | source)
XLA Modules:
  0.0 391.7 jit_solution(11947656834468680656)
XLA Ops:
  7.9 3.0 collective-permute-start
  10.9 5.5 %collective-permute-done = bf16[64,512]{1,0:T(8,128)(2,1)S(1)} collective-permute-done((bf16[64,512]{1,0:T(8,128)(2,1)}, bf16[64,512]{1,0:T(8,128)(2,1)S(1)}, u32[]{:S(2)}, u32[]{:S(2)}) %collective-permute-start) | collective-permute-done | bytes 65568 | tf_op jit(solution)/shard_map/ppermute | solution.py:26
  16.4 4.7 %collective-permute-start.4 = (bf16[64,512]{1,0:T(8,128)(2,1)}, bf16[64,512]{1,0:T(8,128)(2,1)S(1)}, u32[]{:S(2)}, u32[]{:S(2)}) collective-permute-start(bf16[64,512]{1,0:T(8,128)(2,1)} %param.7), channel_id=1, source_target_pairs={{4,0},{8,4},{12,8},{16,12},{20,16},{24,20},{28,24},{0,28},{5,1},{9... | collective-permute-start | bytes 196616 | tf_op jit(solution)/shard_map/ppermute | solution.py:29
  21.2 2.2 collective-permute-done.1
  24.3 5.1 %collective-permute-start.5 = (bf16[64,512]{1,0:T(8,128)(2,1)S(1)}, bf16[64,512]{1,0:T(8,128)(2,1)S(1)}, u32[]{:S(2)}, u32[]{:S(2)}) collective-permute-start(bf16[64,512]{1,0:T(8,128)(2,1)S(1)} %collective-permute-done.4), channel_id=1, source_target_pairs={{4,0},{8,4},{12,8},{16,12},{20,16},{24,20},{28,24},{0,28},{5,1},{9... | collective-permute-start | bytes 196616 | tf_op jit(solution)/shard_map/ppermute | solution.py:29
  29.5 2.3 collective-permute-done.2
  31.7 5.2 %collective-permute-start.6 = (bf16[64,512]{1,0:T(8,128)(2,1)S(1)}, bf16[64,512]{1,0:T(8,128)(2,1)S(1)}, u32[]{:S(2)}, u32[]{:S(2)}) collective-permute-start(bf16[64,512]{1,0:T(8,128)(2,1)S(1)} %collective-permute-done.5), channel_id=1, source_target_pairs={{4,0},{8,4},{12,8},{16,12},{20,16},{24,20},{28,24},{0,28},{5,1},{9... | collective-permute-start | bytes 196616 | tf_op jit(solution)/shard_map/ppermute | solution.py:29
  36.9 1.8 collective-permute-done.3
  38.7 25.5 %all-gather.2.cloned.1.call-done = bf16[16,256,256]{2,1,0:T(8,128)(2,1)} async-done(((bf16[16,32,256]{2,1,0:T(8,128)(2,1)}), bf16[16,256,256]{2,1,0:T(8,128)(2,1)}) %all-gather.2.cloned.1.call-update) | async-done | bytes 2097168 | tf_op jit(solution)/shard_map/all_gather | solution.py:51
  64.2 2.4 convolution_convert_fusion
  66.5 2.5 copy.21
  69.0 4.6 %all-to-all-start = ((bf16[16,256,256]{2,0,1:T(8,128)(2,1)}), bf16[16,256,256]{2,0,1:T(8,128)(2,1)}, u32[]{:S(2)}, u32[]{:S(2)}) async-start(bf16[16,256,256]{2,0,1:T(8,128)(2,1)} %copy.21), calls=%async_computation | async-start | bytes 4194304 | tf_op jit(solution)/shard_map/all_to_all | solution.py:62
  75.5 1.6 reshape_reshape.3
  77.1 22.3 %all-to-all-done = bf16[16,256,256]{2,0,1:T(8,128)(2,1)} async-done(((bf16[16,256,256]{2,0,1:T(8,128)(2,1)}), bf16[16,256,256]{2,0,1:T(8,128)(2,1)}, u32[]{:S(2)}, u32[]{:S(2)}) %all-to-all-start) | async-done | bytes 2097184 | tf_op jit(solution)/shard_map/all_to_all | solution.py:62
  99.4 1.9 copy.22
  101.3 1.3 copy-done.1
  103.4 2.4 copy.24
  105.8 50.7 %all_to_all.72 = f32[64,64,256]{2,1,0:T(8,128)S(1)} all-to-all(f32[64,64,256]{2,1,0:T(8,128)S(1)} %copy.24), channel_id=1, replica_groups=mesh['dp'=8,'feat'=4] {'feat'}, dimensions={0} | all-to-all | bytes 8388608 | tf_op jit(solution)/shard_map/all_to_all | solution.py:68
  158.1 3.3 fusion.6
  161.4 1.2 copy.26
  162.6 28.2 %all_to_all.73 = bf16[16,256,256]{2,0,1:T(8,128)(2,1)S(1)} all-to-all(bf16[16,256,256]{2,0,1:T(8,128)(2,1)S(1)} %copy.26), channel_id=1, replica_groups=mesh['dp'=8,'feat'=4] {'feat'}, dimensions={1} | all-to-all | bytes 4194304 | tf_op jit(solution)/shard_map/all_to_all | solution.py:70
  192.4 1.2 copy.28
  193.6 28.2 %all_to_all.74 = bf16[64,64,256]{2,1,0:T(8,128)(2,1)S(1)} all-to-all(bf16[64,64,256]{2,1,0:T(8,128)(2,1)S(1)} %copy.28), channel_id=1, replica_groups=mesh['dp'=8,'feat'=4] {'feat'}, dimensions={0} | all-to-all | bytes 4194304 | tf_op jit(solution)/shard_map/all_to_all | solution.py:76
  222.0 1.3 copy-done.3
  223.4 2.8 multiply_bitcast_fusion
  226.1 5.5 %copy.30 = f32[16,256,256]{2,0,1:T(8,128)} copy(f32[16,256,256]{1,2,0:T(8,128)} %multiply_bitcast_fusion) | data formatting | bytes 8388608 | tf_op jit(solution)/shard_map/mul | solution.py:87
  231.7 4.3 %convolution_multiply_fusion = f32[64,64,64]{2,1,0:T(8,128)} fusion(bf16[64,64,256]{2,0,1:T(8,128)(2,1)} %bitcast.69, bf16[64,64,256]{2,0,1:T(8,128)(2,1)} %bitcast.71), kind=kOutput, calls=%fused_computation.21 | convolution fusion | flops 134479872 | bytes 5242880 | tf_op jit(solution)/shard_map/bst,cst->sbc/dot_general | solution.py:74
  235.9 3.0 mul.78
  239.0 4.9 %fusion.10 = bf16[16,256,256]{2,1,0:T(8,128)(2,1)} fusion(bf16[16,256,256]{2,1,0:T(8,128)(2,1)} %bitcast.77, bf16[16,256,256]{2,1,0:T(8,128)(2,1)} %all-gather.2.cloned.1.call-done, bf16[16,256,256]{2,1,0:T(8,128)(2,1)} %bitcast.73), kind=kOutput, calls=%fused_computation.16 | convolution fusion | flops 540016640 | bytes 8388608 | tf_op jit(solution)/shard_map/bot,bio->bit/dot_general | solution.py:79
  243.9 73.3 %reduce-scatter.3.cloned.1.call-done = f32[16,32,256]{2,0,1:T(8,128)} async-done(((f32[16,256,256]{2,0,1:T(8,128)}), f32[16,32,256]{2,0,1:T(8,128)}) %reduce-scatter.3.cloned.1.call-update) | async-done | bytes 524304 | tf_op jit(solution)/shard_map/reduce_scatter | solution.py:92
  317.2 2.1 copy.31
  319.4 65.8 %reduce-scatter.5.cloned.1.call-done = f32[64,512]{1,0:T(8,128)} async-done(((f32[64,4096]{1,0:T(8,128)}), f32[64,512]{1,0:T(8,128)}) %reduce-scatter.5.cloned.1.call-update) | async-done | bytes 131088 | tf_op jit(solution)/shard_map/reduce_scatter | solution.py:91
  (39 shorter events, 7.8 us)
Async XLA Ops:
  7.2 57.0 %copy-start = (bf16[4096,256]{1,0:T(8,128)(2,1)S(1)}, bf16[4096,256]{1,0:T(8,128)(2,1)}, u32[]{:S(2)}) copy-start(bf16[4096,256]{1,0:T(8,128)(2,1)} %param.4) | copy-start | bytes 6291460
  7.2 57.0 %all-gather.2.cloned.1.call-start = ((), (), s32[]{:S(2)}) async-start(), calls=%async_computation.6 | async-start | bytes 2359296 | tf_op jit(solution)/shard_map/all_gather | solution.py:51
  7.9 8.5 %collective-permute-start = (bf16[64,512]{1,0:T(8,128)(2,1)}, bf16[64,512]{1,0:T(8,128)(2,1)S(1)}, u32[]{:S(2)}, u32[]{:S(2)}) collective-permute-start(bf16[64,512]{1,0:T(8,128)(2,1)} %param.7), channel_id=1, source_target_pairs={{0,4},{4,8},{8,12},{12,16},{16,20},{20,24},{24,28},{28,0},{1,5},{5... | collective-permute-start | bytes 196616 | tf_op jit(solution)/shard_map/ppermute | solution.py:26
  16.4 7.0 %collective-permute-start.1 = (bf16[64,512]{1,0:T(8,128)(2,1)S(1)}, bf16[64,512]{1,0:T(8,128)(2,1)S(1)}, u32[]{:S(2)}, u32[]{:S(2)}) collective-permute-start(bf16[64,512]{1,0:T(8,128)(2,1)S(1)} %collective-permute-done), channel_id=1, source_target_pairs={{0,4},{4,8},{8,12},{12,16},{16,20},{20,24},{24,28},{28,0},{1,5},{5... | collective-permute-start | bytes 196616 | tf_op jit(solution)/shard_map/ppermute | solution.py:26
  16.4 7.9 %collective-permute-start.4 = (bf16[64,512]{1,0:T(8,128)(2,1)}, bf16[64,512]{1,0:T(8,128)(2,1)S(1)}, u32[]{:S(2)}, u32[]{:S(2)}) collective-permute-start(bf16[64,512]{1,0:T(8,128)(2,1)} %param.7), channel_id=1, source_target_pairs={{4,0},{8,4},{12,8},{16,12},{20,16},{24,20},{28,24},{0,28},{5,1},{9... | collective-permute-start | bytes 196616 | tf_op jit(solution)/shard_map/ppermute | solution.py:29
  23.4 8.3 %collective-permute-start.2 = (bf16[64,512]{1,0:T(8,128)(2,1)S(1)}, bf16[64,512]{1,0:T(8,128)(2,1)S(1)}, u32[]{:S(2)}, u32[]{:S(2)}) collective-permute-start(bf16[64,512]{1,0:T(8,128)(2,1)S(1)} %collective-permute-done.1), channel_id=1, source_target_pairs={{0,4},{4,8},{8,12},{12,16},{16,20},{20,24},{24,28},{28,0},{1,5},{5... | collective-permute-start | bytes 196616 | tf_op jit(solution)/shard_map/ppermute | solution.py:26
  24.3 7.4 %collective-permute-start.5 = (bf16[64,512]{1,0:T(8,128)(2,1)S(1)}, bf16[64,512]{1,0:T(8,128)(2,1)S(1)}, u32[]{:S(2)}, u32[]{:S(2)}) collective-permute-start(bf16[64,512]{1,0:T(8,128)(2,1)S(1)} %collective-permute-done.4), channel_id=1, source_target_pairs={{4,0},{8,4},{12,8},{16,12},{20,16},{24,20},{28,24},{0,28},{5,1},{9... | collective-permute-start | bytes 196616 | tf_op jit(solution)/shard_map/ppermute | solution.py:29
  31.7 7.0 %collective-permute-start.3 = (bf16[64,512]{1,0:T(8,128)(2,1)S(1)}, bf16[64,512]{1,0:T(8,128)(2,1)S(1)}, u32[]{:S(2)}, u32[]{:S(2)}) collective-permute-start(bf16[64,512]{1,0:T(8,128)(2,1)S(1)} %collective-permute-done.2), channel_id=1, source_target_pairs={{0,4},{4,8},{8,12},{12,16},{16,20},{20,24},{24,28},{28,0},{1,5},{5... | collective-permute-start | bytes 196616 | tf_op jit(solution)/shard_map/ppermute | solution.py:26
  31.7 42.0 %collective-permute-start.6 = (bf16[64,512]{1,0:T(8,128)(2,1)S(1)}, bf16[64,512]{1,0:T(8,128)(2,1)S(1)}, u32[]{:S(2)}, u32[]{:S(2)}) collective-permute-start(bf16[64,512]{1,0:T(8,128)(2,1)S(1)} %collective-permute-done.5), channel_id=1, source_target_pairs={{4,0},{8,4},{12,8},{16,12},{20,16},{24,20},{28,24},{0,28},{5,1},{9... | collective-permute-start | bytes 196616 | tf_op jit(solution)/shard_map/ppermute | solution.py:29
  69.0 4.7 %copy-start.5 = (bf16[64,512]{1,0:T(8,128)(2,1)S(1)}, bf16[64,512]{1,0:T(8,128)(2,1)}, u32[]{:S(2)}) copy-start(bf16[64,512]{1,0:T(8,128)(2,1)} %param.7) | copy-start | bytes 196612
  69.0 30.4 %all-to-all-start = ((bf16[16,256,256]{2,0,1:T(8,128)(2,1)}), bf16[16,256,256]{2,0,1:T(8,128)(2,1)}, u32[]{:S(2)}, u32[]{:S(2)}) async-start(bf16[16,256,256]{2,0,1:T(8,128)(2,1)} %copy.21), calls=%async_computation | async-start | bytes 4194304 | tf_op jit(solution)/shard_map/all_to_all | solution.py:62
  73.6 243.6 %reduce-scatter.3.cloned.1.call-start = ((), (), s32[]{:S(2)}) async-start(), calls=%async_computation.7 | async-start | bytes 4718592 | tf_op jit(solution)/shard_map/reduce_scatter | solution.py:92
  101.3 1.3 copy-start.1
  156.5 1.6 copy-start.4
  191.1 1.4 copy-start.2
  222.0 1.3 copy-start.3
  231.6 153.6 %reduce-scatter.5.cloned.1.call-start = ((), (), s32[]{:S(2)}) async-start(), calls=%async_computation.8 | async-start | bytes 1179648 | tf_op jit(solution)/shard_map/reduce_scatter | solution.py:91
Sparse Core Ops, SparseCore 0:
  10.2 53.9 all-gather.1
  231.7 85.4 reduce-scatter.2
  321.6 63.5 reduce-scatter.4
